TPU v7x, 128 devices: a whole 4x4x4 slice. The times are simulated.
128 devices in a mesh: expert: 32 (over y, z, core), ffn: 4 (over x).
Axes of the slice: x: 4, y: 4, z: 4, core: 2. Of those that a mesh axis runs over, the one named last changes fastest.
Arguments:
- tokens: bfloat16 [16384, 768], P('expert', 'ffn'), may hold values from -6 to 6
- cotangent: bfloat16 [16384, 768], P('expert', 'ffn'), may hold values from -6 to 6
- gates: float32 [16384, 2], P('expert'), may hold values from 0.2 to 1
- expert_ids: int32 [16384, 2], P('expert'), may hold values from 0 to 63, all different within a row; in each aligned block of 512 rows (0 to 511, 512 to 1023, ...) at most 32 rows name the same one
- up_weight: bfloat16 [64, 768, 3072], P('expert', None, 'ffn'), may hold values from -0.21875 to 0.21875
- down_weight: bfloat16 [64, 3072, 768], P('expert', 'ffn'), may hold values from -0.109375 to 0.109375
Outputs:
- layer_out: bfloat16 [16384, 768], P('expert', 'ffn')
- grad_tokens: bfloat16 [16384, 768], P('expert', 'ffn')
- grad_up: bfloat16 [64, 768, 3072], P('expert', None, 'ffn')
- grad_down: bfloat16 [64, 3072, 768], P('expert', 'ffn')
Inputs may be any that keep to these rules, and one draw needn't show every extreme that they name: `expert_ids`: the two experts of a token differ. Among the tokens of one index of expert no expert is named more than 32 times, a bound that some block reaches.
All inputs are finite; a program needn't handle non-finite values.
Results may differ from a plain program's by a relative error of at most 0.0065.
Values may be sent and summed in bfloat16 or wider, within the bound.
No kernel may reach another device: no remote copies, remote signals or barrier semaphores. Data moves between devices by JAX's collectives and lax.ppermute only.
A program may use at most 192 MiB of HBM per device.

v0:
```python
import jax
import jax.numpy as jnp
from jax import lax
from jax.experimental.layout import Layout, with_layout_constraint
from jax.sharding import PartitionSpec as P


def slot_targets(expert_ids, owners, local_experts, capacity):
    flat_ids = expert_ids.reshape(-1)
    count = flat_ids.shape[0]
    experts = owners * local_experts
    columns = lax.broadcasted_iota(jnp.int32, (count, experts), 1)
    onehot = (flat_ids[:, None] == columns).astype(jnp.bfloat16)
    earlier = (
        lax.broadcasted_iota(jnp.int32, (count, count), 0)
        > lax.broadcasted_iota(jnp.int32, (count, count), 1)
    ).astype(jnp.bfloat16)
    before = jnp.dot(earlier, onehot, preferred_element_type=jnp.float32)
    position = jnp.sum(onehot.astype(jnp.float32) * before, axis=1).astype(jnp.int32)
    return (flat_ids % local_experts) * (owners * capacity) + (flat_ids // local_experts) * capacity + position


def shards(tokens, cotangent, gates, expert_ids, up_weight, down_weight):
    owners = lax.axis_size("expert")
    local_experts = up_weight.shape[0]
    experts = owners * local_experts
    tok_rows = tokens.shape[0]
    capacity = 2 * tok_rows // owners
    rows = experts * capacity
    slots = owners * capacity
    target = slot_targets(expert_ids, owners, local_experts, capacity)
    row_ids = lax.broadcasted_iota(jnp.int32, (rows, 2 * tok_rows), 0)
    placer = (row_ids == target[None, :]).astype(jnp.bfloat16)
    tok_ids = lax.broadcasted_iota(jnp.int32, (rows, tok_rows), 0)
    pair = target.reshape(tok_rows, 2)
    token_placer = ((tok_ids == pair[None, :, 0]) | (tok_ids == pair[None, :, 1])).astype(
        jnp.bfloat16
    )
    slot_gates = jnp.dot(
        placer.astype(jnp.float32),
        gates.reshape(-1),
        precision=lax.Precision.HIGHEST,
        preferred_element_type=jnp.float32,
    )

    whole_tokens = lax.all_gather(tokens, "ffn", axis=1, tiled=True)
    whole_cot = lax.all_gather(cotangent, "ffn", axis=1, tiled=True)

    def dispatch(send):
        send = send.reshape(local_experts, owners, capacity, *send.shape[1:])
        got = lax.all_to_all(send, "expert", split_axis=1, concat_axis=1, tiled=True)
        return got.reshape(local_experts, slots, *got.shape[3:])

    def place(whole):
        return jnp.dot(token_placer, whole, preferred_element_type=jnp.float32).astype(
            jnp.bfloat16
        )

    rows_in = dispatch(place(whole_tokens))
    scaled = slot_gates[:, None] * jnp.dot(
        token_placer, whole_cot, preferred_element_type=jnp.float32
    )
    rows_in, grads_send = lax.optimization_barrier((rows_in, scaled.astype(jnp.bfloat16)))
    grads_in = dispatch(grads_send)

    preact = jnp.einsum("xsd,xdf->xsf", rows_in, up_weight, preferred_element_type=jnp.float32)
    gating = jax.nn.sigmoid(preact)
    activated = (preact * gating).astype(jnp.bfloat16)
    out_part = [
        with_layout_constraint(
            jnp.einsum(
                "fd,sf->ds", down_weight[x], activated[x], preferred_element_type=jnp.float32
            ),
            Layout((0, 1)),
        ).astype(jnp.bfloat16)
        for x in range(local_experts)
    ]

    def ring_reduce(parts):
        ffn = lax.axis_size("ffn")
        me = lax.axis_index("ffn")
        sums = []
        for x, part in enumerate(parts):
            way = 1 if x % 2 == 0 else -1
            chunks = part.reshape(ffn, part.shape[0] // ffn, part.shape[1])
            order = (me - way * jnp.arange(1, ffn + 1, dtype=jnp.int32)) % ffn
            chunks = jnp.take(chunks, order, axis=0)
            perm = [(i, (i + way) % ffn) for i in range(ffn)]
            acc = chunks[0].astype(jnp.float32)
            for step in range(1, ffn):
                acc = lax.ppermute(acc.astype(jnp.bfloat16), "ffn", perm).astype(jnp.float32)
                acc = acc + chunks[step].astype(jnp.float32)
            sums.append(acc.astype(jnp.bfloat16))
        return sums

    def send_home(parts, ring):
        if ring:
            cols = jnp.stack(ring_reduce(parts), axis=1)
        else:
            cols = jnp.stack(
                [lax.psum_scatter(p, "ffn", scatter_dimension=0, tiled=True) for p in parts],
                axis=1,
            )
        cols = cols.reshape(cols.shape[0], local_experts, owners, capacity)
        back = lax.all_to_all(cols, "expert", split_axis=2, concat_axis=2, tiled=True)
        return back.reshape(back.shape[0], rows)

    out_home = send_home(out_part, False)
    back_grad = jnp.einsum(
        "xsd,xfd->xsf", grads_in, down_weight, preferred_element_type=jnp.float32
    )
    pre_grad = (back_grad * gating * (1.0 + preact * (1.0 - gating))).astype(jnp.bfloat16)
    grad_down = jnp.einsum(
        "xsf,xsd->xfd", activated, grads_in, preferred_element_type=jnp.float32
    ).astype(jnp.bfloat16)
    grad_up = jnp.einsum(
        "xsd,xsf->xdf", rows_in, pre_grad, preferred_element_type=jnp.float32
    ).astype(jnp.bfloat16)
    in_part = [
        with_layout_constraint(
            jnp.einsum(
                "df,sf->ds", up_weight[x], pre_grad[x], preferred_element_type=jnp.float32
            ),
            Layout((0, 1)),
        ).astype(jnp.bfloat16)
        for x in range(local_experts)
    ]
    in_home = send_home(in_part, True)

    def gather_back(returned):
        picked = jnp.take(returned.T, target, axis=0).astype(jnp.float32)
        return picked.reshape(tok_rows, 2, returned.shape[0])

    layer_out = jnp.sum(gates[:, :, None] * gather_back(out_home), axis=1).astype(jnp.bfloat16)
    grad_tokens = jnp.sum(gather_back(in_home), axis=1).astype(jnp.bfloat16)
    return (layer_out, grad_tokens, grad_up, grad_down)


def solution(mesh):
    placed = (
        P("expert", "ffn"),
        P("expert", "ffn"),
        P("expert", None),
        P("expert", None),
        P("expert", None, "ffn"),
        P("expert", "ffn", None),
    )
    return jax.shard_map(
        shards,
        mesh=mesh,
        in_specs=placed,
        out_specs=(
            P("expert", "ffn"),
            P("expert", "ffn"),
            P("expert", None, "ffn"),
            P("expert", "ffn", None),
        ),
        check_vma=False,
    )
```

profile of v0, /device:TPU:1, one launch (start us, length us, event | category | flops | bytes accessed | tf_op | source)
XLA Modules:
  0.0 243.3 jit_solution(7724069945755014578)
XLA Ops:
  10.5 12.9 %all_gather.6 = bf16[512,768]{0,1:T(8,128)(2,1)S(1)} all-gather(bf16[512,192]{0,1:T(8,128)(2,1)S(1)} %copy-done.4), channel_id=1, replica_groups=mesh['expert'=32,'ffn'=4] {'ffn'}, dimensions={1}, use_global_device_ids=true | all-gather | bytes 983040 | tf_op jit(solution)/shard_map/all_gather | solution.py:46
  27.4 10.5 %all-to-all-start = ((bf16[2,32,32,768]{3,2,0,1:T(8,128)(2,1)}), bf16[2,32,32,768]{3,2,0,1:T(8,128)(2,1)S(1)}, u32[]{:S(2)}, u32[]{:S(2)}) async-start(bf16[2,32,32,768]{3,2,0,1:T(8,128)(2,1)} %copy.56), calls=%async_computation | async-start | bytes 6291456 | tf_op jit(solution)/shard_map/all_to_all | solution.py:51
  38.4 3.7 %fusion = f32[1,2048]{1,0:T(1,128)S(1)} fusion(f32[1024,1]{0,1:T(1,128)S(1)} %reshape.208, s32[1024]{0:T(1024)S(1)} %get-tuple-element.17), kind=kOutput, calls=%fused_computation.5 | convolution fusion | flops 27262976 | bytes 16384 | tf_op jit(solution)/shard_map/dot_general | solution.py:39
  42.1 12.8 %all_gather.7 = bf16[512,768]{0,1:T(8,128)(2,1)S(1)} all-gather(bf16[512,192]{0,1:T(8,128)(2,1)S(1)} %copy-done.5), channel_id=1, replica_groups=mesh['expert'=32,'ffn'=4] {'ffn'}, dimensions={1}, use_global_device_ids=true | all-gather | bytes 983040 | tf_op jit(solution)/shard_map/all_gather | solution.py:47
  54.9 3.8 %multiply_convert_fusion.2 = bf16[2048,768]{1,0:T(8,128)(2,1)} fusion(bf16[512,768]{0,1:T(8,128)(2,1)S(1)} %all_gather.7, f32[2048]{0:T(1024)S(1)} %bitcast.108, s32[512]{0:T(512)S(1)} %get-tuple-element.15, s32[512]{0:T(512)S(1)} %get-tuple-element.14), kind=kOutput, calls=%fused_computation.9 | convolution fusion | flops 1616904192 | bytes 3944448 | tf_op jit(solution)/shard_map/dot_general | solution.py:60
  58.7 19.0 %all-to-all-done = bf16[2,32,32,768]{3,2,0,1:T(8,128)(2,1)S(1)} async-done(((bf16[2,32,32,768]{3,2,0,1:T(8,128)(2,1)}), bf16[2,32,32,768]{3,2,0,1:T(8,128)(2,1)S(1)}, u32[]{:S(2)}, u32[]{:S(2)}) %all-to-all-start) | async-done | bytes 3145760 | tf_op jit(solution)/shard_map/all_to_all | solution.py:51
  80.5 5.0 %multiply_convert_fusion.1 = (bf16[2,1024,768]{2,1,0:T(8,128)(2,1)S(1)}, f32[2,1024,768]{2,1,0:T(8,128)}) fusion(bf16[2,1024,768]{2,1,0:T(8,128)(2,1)S(1)} %bitcast.96, bf16[2,768,768]{2,1,0:T(8,128)(2,1)S(1)} %copy-done.9), kind=kOutput, calls=%fused_computation.7 | convolution fusion | flops 2423783424 | bytes 14942208 | tf_op jit(solution)/shard_map/xsd,xdf->xsf/dot_general | solution.py:66
  87.2 2.6 %bitcast_convert_fusion.2 = bf16[768,1024]{1,0:T(8,128)(2,1)} fusion(bf16[2,1024,768]{2,1,0:T(8,128)(2,1)S(1)} %get-tuple-element.20, bf16[2,768,768]{2,1,0:T(8,128)(2,1)S(1)} %copy-done.7), kind=kOutput, calls=%fused_computation.19 | convolution fusion | flops 1208745984 | bytes 4325376 | tf_op jit(solution)/shard_map/fd,sf->ds/dot_general | solution.py:71
  91.7 4.4 %all-to-all-start.2 = ((bf16[2,32,32,768]{3,2,0,1:T(8,128)(2,1)}), bf16[2,32,32,768]{3,2,0,1:T(8,128)(2,1)S(1)}, u32[]{:S(2)}, u32[]{:S(2)}) async-start(bf16[2,32,32,768]{3,2,0,1:T(8,128)(2,1)} %copy.63), calls=%async_computation.4 | async-start | bytes 6291456 | tf_op jit(solution)/shard_map/all_to_all | solution.py:51
  96.3 4.6 %bitcast_convert_fusion.3 = bf16[768,1024]{1,0:T(8,128)(2,1)} fusion(bf16[2,1024,768]{2,1,0:T(8,128)(2,1)} %copy-done.12, bf16[2,768,768]{2,1,0:T(8,128)(2,1)} %param.15), kind=kOutput, calls=%fused_computation.20 | convolution fusion | flops 1208745984 | bytes 4325376 | tf_op jit(solution)/shard_map/fd,sf->ds/dot_general | solution.py:71
  100.9 35.1 %all-to-all-done.2 = bf16[2,32,32,768]{3,2,0,1:T(8,128)(2,1)S(1)} async-done(((bf16[2,32,32,768]{3,2,0,1:T(8,128)(2,1)}), bf16[2,32,32,768]{3,2,0,1:T(8,128)(2,1)S(1)}, u32[]{:S(2)}, u32[]{:S(2)}) %all-to-all-start.2) | async-done | bytes 3145760 | tf_op jit(solution)/shard_map/all_to_all | solution.py:51
  138.8 5.9 %multiply_convert_fusion = bf16[2,1024,768]{2,1,0:T(8,128)(2,1)S(1)} fusion(f32[2,1024,768]{2,1,0:T(8,128)} %get-tuple-element.21, bf16[2,1024,768]{2,1,0:T(8,128)(2,1)S(1)} %bitcast.98, bf16[2,768,768]{2,1,0:T(8,128)(2,1)S(1)} %copy-done.8), kind=kOutput, calls=%fused_computation.6 | convolution fusion | flops 2430074880 | bytes 14942208 | tf_op jit(solution)/shard_map/xsd,xfd->xsf/dot_general | solution.py:109
  149.7 2.8 %bitcast_convert_fusion = bf16[768,1024]{1,0:T(8,128)(2,1)S(1)} fusion(bf16[2,1024,768]{2,1,0:T(8,128)(2,1)} %copy-done.14, bf16[2,768,768]{2,1,0:T(8,128)(2,1)S(1)} %copy-done.11), kind=kOutput, calls=%fused_computation.17 | convolution fusion | flops 1208745984 | bytes 4325376 | tf_op jit(solution)/shard_map/df,sf->ds/dot_general | solution.py:121
  161.9 3.9 %collective-permute-done.3 = bf16[192,1024]{1,0:T(8,128)(2,1)S(1)} collective-permute-done((bf16[192,1024]{1,0:T(8,128)(2,1)S(1)}, bf16[192,1024]{1,0:T(8,128)(2,1)S(1)}, u32[]{:S(2)}, u32[]{:S(2)}) %collective-permute-start.3) | collective-permute-done | bytes 393248 | tf_op jit(solution)/shard_map/ppermute | solution.py:91
  166.7 3.4 %collective-permute-start.4 = (bf16[192,1024]{1,0:T(8,128)(2,1)}, bf16[192,1024]{1,0:T(8,128)(2,1)}, u32[]{:S(2)}, u32[]{:S(2)}) collective-permute-start(bf16[192,1024]{1,0:T(8,128)(2,1)} %fusion.22), channel_id=1, source_target_pairs={{0,3},{1,0},{2,1},{3,2},{4,7},{5,4},{6,5},{7,6},{8,11},{9,8},{10,9... | collective-permute-start | bytes 1179656 | tf_op jit(solution)/shard_map/ppermute | solution.py:91
  176.5 6.1 %all-to-all-start.1 = ((bf16[192,2,32,32]{0,3,1,2:T(8,128)(2,1)}), bf16[192,2,32,32]{0,3,1,2:T(8,128)(2,1)}, u32[]{:S(2)}, u32[]{:S(2)}) async-start(bf16[192,2,32,32]{0,3,1,2:T(8,128)(2,1)} %copy.61), calls=%async_computation.3 | async-start | bytes 2097152 | tf_op jit(solution)/shard_map/all_to_all | solution.py:105
  185.8 2.7 %collective-permute-start.5 = (bf16[192,1024]{1,0:T(8,128)(2,1)}, bf16[192,1024]{1,0:T(8,128)(2,1)}, u32[]{:S(2)}, u32[]{:S(2)}) collective-permute-start(bf16[192,1024]{1,0:T(8,128)(2,1)} %fusion.21), channel_id=1, source_target_pairs={{0,3},{1,0},{2,1},{3,2},{4,7},{5,4},{6,5},{7,6},{8,11},{9,8},{10,9... | collective-permute-start | bytes 1179656 | tf_op jit(solution)/shard_map/ppermute | solution.py:91
  188.4 7.0 %collective-permute-done.2 = bf16[192,1024]{1,0:T(8,128)(2,1)S(1)} collective-permute-done((bf16[192,1024]{1,0:T(8,128)(2,1)S(1)}, bf16[192,1024]{1,0:T(8,128)(2,1)S(1)}, u32[]{:S(2)}, u32[]{:S(2)}) %collective-permute-start.2) | collective-permute-done | bytes 393248 | tf_op jit(solution)/shard_map/ppermute | solution.py:91
  200.2 8.3 %all-to-all-start.3 = ((bf16[192,2,32,32]{0,3,1,2:T(8,128)(2,1)}), bf16[192,2,32,32]{0,3,1,2:T(8,128)(2,1)S(1)}, u32[]{:S(2)}, u32[]{:S(2)}) async-start(bf16[192,2,32,32]{0,3,1,2:T(8,128)(2,1)} %copy.67), calls=%async_computation.5 | async-start | bytes 2097152 | tf_op jit(solution)/shard_map/all_to_all | solution.py:105
  208.5 7.1 %convolution_convert_fusion.2 = bf16[2,768,768]{2,1,0:T(8,128)(2,1)} fusion(bf16[2,1024,768]{2,1,0:T(8,128)(2,1)} %bitcast.97, bf16[2,1024,768]{2,1,0:T(8,128)(2,1)} %copy-done.14), kind=kOutput, calls=%fused_computation.26 | convolution fusion | flops 2417098752 | bytes 8650752 | tf_op jit(solution)/shard_map/xsd,xsf->xdf/dot_general | solution.py:116
  215.6 4.1 %convolution_convert_fusion.1 = bf16[2,768,768]{2,1,0:T(8,128)(2,1)} fusion(bf16[2,1024,768]{2,1,0:T(8,128)(2,1)S(1)} %copy-done.13, bf16[2,1024,768]{2,1,0:T(8,128)(2,1)S(1)} %bitcast.99), kind=kOutput, calls=%fused_computation.25 | convolution fusion | flops 2417098752 | bytes 8650752 | tf_op jit(solution)/shard_map/xsf,xsd->xfd/dot_general | solution.py:113
  221.0 3.9 %gather_fusion = bf16[1024,192]{1,0:T(8,128)(2,1)S(1)} fusion(bf16[2048,192]{1,0:T(8,128)(2,1)S(1)} %bitcast.95, s32[1024]{0:T(1024)S(1)} %fusion.44), kind=kCustom, calls=%fused_computation.clone | custom fusion | bytes 790528 | tf_op jit(solution)/shard_map/jit(_take)/gather | solution.py:131
  225.5 3.9 %gather_fusion.3 = bf16[1024,192]{1,0:T(8,128)(2,1)S(1)} fusion(bf16[2048,192]{1,0:T(8,128)(2,1)S(1)} %bitcast.94, s32[1024]{0:T(1024)S(1)} %fusion.44), kind=kCustom, calls=%fused_computation.2.clone | custom fusion | bytes 790528 | tf_op jit(solution)/shard_map/jit(_take)/gather | solution.py:131
  230.3 2.9 %multiply_reduce_fusion = bf16[512,192]{1,0:T(8,128)(2,1)S(1)} fusion(f32[512,2,192]{2,1,0:T(2,128)S(1)} %reshape.157, f32[512,2]{1,0:T(8,128)S(1)} %copy.47), kind=kLoop, calls=%fused_computation.45 | loop fusion | flops 294912 | bytes 987136 | tf_op jit(solution)/shard_map/reduce_sum | solution.py:134
  (97 shorter events, 52.5 us)
Async XLA Ops:
  7.2 3.4 %copy-start.4 = (bf16[512,192]{0,1:T(8,128)(2,1)S(1)}, bf16[512,192]{0,1:T(8,128)(2,1)}, u32[]{:S(2)}) copy-start(bf16[512,192]{0,1:T(8,128)(2,1)} %param.10) | copy-start | bytes 589828
  27.4 10.6 %copy-start.6 = (f32[512,2]{0,1:T(2,128)S(1)}, f32[512,2]{0,1:T(2,128)}, u32[]{:S(2)}) copy-start(f32[512,2]{0,1:T(2,128)} %param.12) | copy-start | bytes 12292
  27.4 50.2 %all-to-all-start = ((bf16[2,32,32,768]{3,2,0,1:T(8,128)(2,1)}), bf16[2,32,32,768]{3,2,0,1:T(8,128)(2,1)S(1)}, u32[]{:S(2)}, u32[]{:S(2)}) async-start(bf16[2,32,32,768]{3,2,0,1:T(8,128)(2,1)} %copy.56), calls=%async_computation | async-start | bytes 6291456 | tf_op jit(solution)/shard_map/all_to_all | solution.py:51
  37.9 132.1 %reduce-scatter.5.cloned.1.call-start = ((), (), s32[]{:S(2)}) async-start(), calls=%async_computation.7 | async-start | bytes 1966080 | tf_op jit(solution)/shard_map/reduce_scatter | solution.py:101
  38.3 3.8 %copy-start.5 = (bf16[512,192]{0,1:T(8,128)(2,1)S(1)}, bf16[512,192]{0,1:T(8,128)(2,1)}, u32[]{:S(2)}) copy-start(bf16[512,192]{0,1:T(8,128)(2,1)} %param.11) | copy-start | bytes 589828
  77.7 2.8 %copy-start.9 = (bf16[2,768,768]{2,1,0:T(8,128)(2,1)S(1)}, bf16[2,768,768]{2,1,0:T(8,128)(2,1)}, u32[]{:S(2)}) copy-start(bf16[2,768,768]{2,1,0:T(8,128)(2,1)} %param.14) | copy-start | bytes 7077892
  77.9 7.5 %copy-start = (bf16[2,32,32,768]{3,2,1,0:T(8,128)(2,1)}, bf16[2,32,32,768]{3,2,1,0:T(8,128)(2,1)S(1)}, u32[]{:S(2)}) copy-start(bf16[2,32,32,768]{3,2,1,0:T(8,128)(2,1)S(1)} %copy.57) | copy-start | bytes 9437188
  80.4 6.7 %copy-start.7 = (bf16[2,768,768]{2,1,0:T(8,128)(2,1)S(1)}, bf16[2,768,768]{2,1,0:T(8,128)(2,1)}, u32[]{:S(2)}) copy-start(bf16[2,768,768]{2,1,0:T(8,128)(2,1)} %param.15) | copy-start | bytes 7077892
  91.7 44.2 %all-to-all-start.2 = ((bf16[2,32,32,768]{3,2,0,1:T(8,128)(2,1)}), bf16[2,32,32,768]{3,2,0,1:T(8,128)(2,1)S(1)}, u32[]{:S(2)}, u32[]{:S(2)}) async-start(bf16[2,32,32,768]{3,2,0,1:T(8,128)(2,1)} %copy.63), calls=%async_computation.4 | async-start | bytes 6291456 | tf_op jit(solution)/shard_map/all_to_all | solution.py:51
  96.2 75.9 %reduce-scatter.3.cloned.1.call-start = ((), (), s32[]{:S(2)}) async-start(), calls=%async_computation.6 | async-start | bytes 1966080 | tf_op jit(solution)/shard_map/reduce_scatter | solution.py:101
  136.0 2.8 %copy-start.8 = (bf16[2,768,768]{2,1,0:T(8,128)(2,1)S(1)}, bf16[2,768,768]{2,1,0:T(8,128)(2,1)}, u32[]{:S(2)}) copy-start(bf16[2,768,768]{2,1,0:T(8,128)(2,1)} %param.15) | copy-start | bytes 7077892
  136.2 8.5 %copy-start.1 = (bf16[2,32,32,768]{3,2,1,0:T(8,128)(2,1)}, bf16[2,32,32,768]{3,2,1,0:T(8,128)(2,1)S(1)}, u32[]{:S(2)}) copy-start(bf16[2,32,32,768]{3,2,1,0:T(8,128)(2,1)S(1)} %copy.64) | copy-start | bytes 9437188
  138.8 5.9 %copy-start.10 = (bf16[2,768,768]{2,1,0:T(8,128)(2,1)S(1)}, bf16[2,768,768]{2,1,0:T(8,128)(2,1)}, u32[]{:S(2)}) copy-start(bf16[2,768,768]{2,1,0:T(8,128)(2,1)} %param.14) | copy-start | bytes 7077892
  147.0 2.7 %copy-start.11 = (bf16[2,768,768]{2,1,0:T(8,128)(2,1)S(1)}, bf16[2,768,768]{2,1,0:T(8,128)(2,1)}, u32[]{:S(2)}) copy-start(bf16[2,768,768]{2,1,0:T(8,128)(2,1)} %param.14) | copy-start | bytes 7077892
  148.0 11.8 %collective-permute-start = (bf16[192,1024]{1,0:T(8,128)(2,1)}, bf16[192,1024]{1,0:T(8,128)(2,1)}, u32[]{:S(2)}, u32[]{:S(2)}) collective-permute-start(bf16[192,1024]{1,0:T(8,128)(2,1)} %slice_bitcast_fusion.15), channel_id=1, source_target_pairs={{0,1},{1,2},{2,3},{3,0},{4,5},{5,6},{6,7},{7,4},{8,9},{9,10},{10,1... | collective-permute-start | bytes 1179656 | tf_op jit(solution)/shard_map/ppermute | solution.py:91
  156.0 9.8 %collective-permute-start.3 = (bf16[192,1024]{1,0:T(8,128)(2,1)S(1)}, bf16[192,1024]{1,0:T(8,128)(2,1)S(1)}, u32[]{:S(2)}, u32[]{:S(2)}) collective-permute-start(bf16[192,1024]{1,0:T(8,128)(2,1)S(1)} %slice_bitcast_fusion.11), channel_id=1, source_target_pairs={{0,3},{1,0},{2,1},{3,2},{4,7},{5,4},{6,5},{7,6},{8,11},{9,8},{10,9... | collective-permute-start | bytes 1179656 | tf_op jit(solution)/shard_map/ppermute | solution.py:91
  161.7 20.9 %collective-permute-start.1 = (bf16[192,1024]{1,0:T(8,128)(2,1)}, bf16[192,1024]{1,0:T(8,128)(2,1)}, u32[]{:S(2)}, u32[]{:S(2)}) collective-permute-start(bf16[192,1024]{1,0:T(8,128)(2,1)} %fusion.25), channel_id=1, source_target_pairs={{0,1},{1,2},{2,3},{3,0},{4,5},{5,6},{6,7},{7,4},{8,9},{9,10},{10,1... | collective-permute-start | bytes 1179656 | tf_op jit(solution)/shard_map/ppermute | solution.py:91
  166.7 17.2 %collective-permute-start.4 = (bf16[192,1024]{1,0:T(8,128)(2,1)}, bf16[192,1024]{1,0:T(8,128)(2,1)}, u32[]{:S(2)}, u32[]{:S(2)}) collective-permute-start(bf16[192,1024]{1,0:T(8,128)(2,1)} %fusion.22), channel_id=1, source_target_pairs={{0,3},{1,0},{2,1},{3,2},{4,7},{5,4},{6,5},{7,6},{8,11},{9,8},{10,9... | collective-permute-start | bytes 1179656 | tf_op jit(solution)/shard_map/ppermute | solution.py:91
  176.5 23.7 %all-to-all-start.1 = ((bf16[192,2,32,32]{0,3,1,2:T(8,128)(2,1)}), bf16[192,2,32,32]{0,3,1,2:T(8,128)(2,1)}, u32[]{:S(2)}, u32[]{:S(2)}) async-start(bf16[192,2,32,32]{0,3,1,2:T(8,128)(2,1)} %copy.61), calls=%async_computation.3 | async-start | bytes 2097152 | tf_op jit(solution)/shard_map/all_to_all | solution.py:105
  183.8 11.6 %collective-permute-start.2 = (bf16[192,1024]{1,0:T(8,128)(2,1)S(1)}, bf16[192,1024]{1,0:T(8,128)(2,1)S(1)}, u32[]{:S(2)}, u32[]{:S(2)}) collective-permute-start(bf16[192,1024]{1,0:T(8,128)(2,1)S(1)} %fusion.24), channel_id=1, source_target_pairs={{0,1},{1,2},{2,3},{3,0},{4,5},{5,6},{6,7},{7,4},{8,9},{9,10},{10,1... | collective-permute-start | bytes 1179656 | tf_op jit(solution)/shard_map/ppermute | solution.py:91
  185.8 11.8 %collective-permute-start.5 = (bf16[192,1024]{1,0:T(8,128)(2,1)}, bf16[192,1024]{1,0:T(8,128)(2,1)}, u32[]{:S(2)}, u32[]{:S(2)}) collective-permute-start(bf16[192,1024]{1,0:T(8,128)(2,1)} %fusion.21), channel_id=1, source_target_pairs={{0,3},{1,0},{2,1},{3,2},{4,7},{5,4},{6,5},{7,6},{8,11},{9,8},{10,9... | collective-permute-start | bytes 1179656 | tf_op jit(solution)/shard_map/ppermute | solution.py:91
  200.2 25.2 %all-to-all-start.3 = ((bf16[192,2,32,32]{0,3,1,2:T(8,128)(2,1)}), bf16[192,2,32,32]{0,3,1,2:T(8,128)(2,1)S(1)}, u32[]{:S(2)}, u32[]{:S(2)}) async-start(bf16[192,2,32,32]{0,3,1,2:T(8,128)(2,1)} %copy.67), calls=%async_computation.5 | async-start | bytes 2097152 | tf_op jit(solution)/shard_map/all_to_all | solution.py:105
  208.5 7.1 %copy-start.2 = (bf16[2,32,32,768]{3,2,1,0:T(8,128)(2,1)S(1)}, bf16[2,32,32,768]{3,2,1,0:T(8,128)(2,1)}, u32[]{:S(2)}) copy-start(bf16[2,32,32,768]{3,2,1,0:T(8,128)(2,1)} %copy-done.1) | copy-start | bytes 9437188
  208.5 7.1 %copy-start.13 = (bf16[2,1024,768]{2,1,0:T(8,128)(2,1)S(1)}, bf16[2,1024,768]{2,1,0:T(8,128)(2,1)}, u32[]{:S(2)}) copy-start(bf16[2,1024,768]{2,1,0:T(8,128)(2,1)} %copy-done.12) | copy-start | bytes 9437188
  (3 other events, 6.0 us)
Sparse Core Ops, SparseCore 0:
  89.9 22.9 reduce-scatter.4
  115.3 25.3 reduce-scatter.2
where the time goes:
time: 244 us; the launch traced here: 243 us
  waiting for transfers between devices  67.4 us (28%)
  matrix products  43.7 us (18%)
  starting transfers between devices  39.3 us (16%)
  local copies, waits for them, and re-layouts  36 us (15%)
  blocking collectives  25.6 us (10%)
  other arithmetic  16.9 us (7%)
  between operations  14.5 us (6%)
    all_to_all x2, waiting for transfers between devices, dispatch(): lax.all_to_all(send, 'expert', split_axis=1, concat_axis=1, tiled=True)  54.1 us
    all_to_all x2, starting transfers between devices, dispatch(): lax.all_to_all(send, 'expert', split_axis=1, concat_axis=1, tiled=True)  14.9 us
    all_to_all x2, starting transfers between devices, send_home(): lax.all_to_all(cols, 'expert', split_axis=2, concat_axis=2, tiled=True)  14.4 us
    all_gather x1, blocking collectives, shards(): whole_tokens = lax.all_gather(tokens, 'ffn', axis=1, tiled=True)  12.9 us
    ppermute x6, waiting for transfers between devices, ring_reduce(): lax.ppermute(acc.astype(jnp.bfloat16), 'ffn', perm).astype(jnp.float32)  12.8 us
    all_gather x1, blocking collectives, shards(): whole_cot = lax.all_gather(cotangent, 'ffn', axis=1, tiled=True)  12.8 us
    ppermute x6, starting transfers between devices, ring_reduce(): lax.ppermute(acc.astype(jnp.bfloat16), 'ffn', perm).astype(jnp.float32)  9.96 us
    unnamed x34, local copies, waits for them, and re-layouts  9.7 us
  transfers between devices with their start and end apart: 12, of which 6 were waited for; matrix products, arithmetic and copies ran while one was open for 26% of the time, Pallas kernels for 0%

commit v1 on v0

--- a/solution.py
+++ b/solution.py
@@ -93,19 +93,20 @@
             sums.append(acc.astype(jnp.bfloat16))
         return sums
 
-    def send_home(parts, ring):
+    def reduce_home(parts, ring):
         if ring:
-            cols = jnp.stack(ring_reduce(parts), axis=1)
-        else:
-            cols = jnp.stack(
-                [lax.psum_scatter(p, "ffn", scatter_dimension=0, tiled=True) for p in parts],
-                axis=1,
-            )
-        cols = cols.reshape(cols.shape[0], local_experts, owners, capacity)
-        back = lax.all_to_all(cols, "expert", split_axis=2, concat_axis=2, tiled=True)
-        return back.reshape(back.shape[0], rows)
+            return jnp.stack(ring_reduce(parts), axis=1)
+        return jnp.stack(
+            [lax.psum_scatter(p, "ffn", scatter_dimension=0, tiled=True) for p in parts],
+            axis=1,
+        )
 
-    out_home = send_home(out_part, False)
+    def send_home(both):
+        both = both.reshape(*both.shape[:3], owners, capacity)
+        back = lax.all_to_all(both, "expert", split_axis=3, concat_axis=3, tiled=True)
+        return back.reshape(*back.shape[:2], rows)
+
+    out_cols = reduce_home(out_part, False)
     back_grad = jnp.einsum(
         "xsd,xfd->xsf", grads_in, down_weight, preferred_element_type=jnp.float32
     )
@@ -125,7 +126,8 @@
         ).astype(jnp.bfloat16)
         for x in range(local_experts)
     ]
-    in_home = send_home(in_part, True)
+    in_cols = reduce_home(in_part, True)
+    out_home, in_home = send_home(jnp.stack([out_cols, in_cols]))
 
     def gather_back(returned):
         picked = jnp.take(returned.T, target, axis=0).astype(jnp.float32)

time: 244 us -> 254 us (1.041)
  waiting for transfers between devices: 67.4 us -> 83.7 us
  starting transfers between devices: 39.3 us -> 33.2 us
    all_to_all x2 -> x1, waiting for transfers between devices: 0.45 us -> 17.1 us  [send_home(): lax.all_to_all(both, 'expert', split_axis=3, concat_axis=3, tiled=True)]
    all_to_all x2 -> x1, starting transfers between devices: 14.4 us -> 7.45 us  [send_home(): lax.all_to_all(both, 'expert', split_axis=3, concat_axis=3, tiled=True)]
    convert_element_type x4, other arithmetic: 5.79 us -> 3.05 us  [ring_reduce(): acc.astype(jnp.bfloat16)]
    unnamed x34 -> x38, local copies, waits for them, and re-layouts: 9.7 us -> 9.69 us
  transfers between devices with their start and end apart: 12 -> 11, of which waited for: 6 -> 7; matrix products, arithmetic and copies ran while one was open for 26% -> 20% of each run, Pallas kernels for 0% -> 0%
where the time goes in v1:
time: 254 us; the launch traced here: 253 us
  waiting for transfers between devices  83.7 us (33%)
  matrix products  43.6 us (17%)
  local copies, waits for them, and re-layouts  36.4 us (14%)
  starting transfers between devices  33.2 us (13%)
  blocking collectives  25.6 us (10%)
  other arithmetic  15.8 us (6%)
  between operations  14.5 us (6%)
    all_to_all x2, waiting for transfers between devices, dispatch(): lax.all_to_all(send, 'expert', split_axis=1, concat_axis=1, tiled=True)  54.1 us
    all_to_all x1, waiting for transfers between devices, send_home(): lax.all_to_all(both, 'expert', split_axis=3, concat_axis=3, tiled=True)  17.1 us
    all_to_all x2, starting transfers between devices, dispatch(): lax.all_to_all(send, 'expert', split_axis=1, concat_axis=1, tiled=True)  14.9 us
    all_gather x1, blocking collectives, shards(): whole_tokens = lax.all_gather(tokens, 'ffn', axis=1, tiled=True)  12.9 us
    all_gather x1, blocking collectives, shards(): whole_cot = lax.all_gather(cotangent, 'ffn', axis=1, tiled=True)  12.8 us
    ppermute x6, waiting for transfers between devices, ring_reduce(): lax.ppermute(acc.astype(jnp.bfloat16), 'ffn', perm).astype(jnp.float32)  12.4 us
    ppermute x6, starting transfers between devices, ring_reduce(): lax.ppermute(acc.astype(jnp.bfloat16), 'ffn', perm).astype(jnp.float32)  10.8 us
    unnamed x38, local copies, waits for them, and re-layouts  9.69 us
  transfers between devices with their start and end apart: 11, of which 7 were waited for; matrix products, arithmetic and copies ran while one was open for 20% of the time, Pallas kernels for 0%

profile of v1, /device:TPU:1, one launch (start us, length us, event | category | flops | bytes accessed | tf_op | source)
XLA Modules:
  0.0 252.9 jit_solution(2167192281950988621)
XLA Ops:
  10.5 12.9 %all_gather.6 = bf16[512,768]{0,1:T(8,128)(2,1)S(1)} all-gather(bf16[512,192]{0,1:T(8,128)(2,1)S(1)} %copy-done.6), channel_id=1, replica_groups=mesh['expert'=32,'ffn'=4] {'ffn'}, dimensions={1}, use_global_device_ids=true | all-gather | bytes 983040 | tf_op jit(solution)/shard_map/all_gather | solution.py:46
  27.4 10.5 %all-to-all-start = ((bf16[2,32,32,768]{3,2,0,1:T(8,128)(2,1)}), bf16[2,32,32,768]{3,2,0,1:T(8,128)(2,1)S(1)}, u32[]{:S(2)}, u32[]{:S(2)}) async-start(bf16[2,32,32,768]{3,2,0,1:T(8,128)(2,1)} %copy.55), calls=%async_computation | async-start | bytes 6291456 | tf_op jit(solution)/shard_map/all_to_all | solution.py:51
  38.4 3.7 %fusion = f32[1,2048]{1,0:T(1,128)S(1)} fusion(f32[1024,1]{0,1:T(1,128)S(1)} %reshape.208, s32[1024]{0:T(1024)S(1)} %get-tuple-element.17), kind=kOutput, calls=%fused_computation.5 | convolution fusion | flops 27262976 | bytes 16384 | tf_op jit(solution)/shard_map/dot_general | solution.py:39
  42.1 12.8 %all_gather.7 = bf16[512,768]{0,1:T(8,128)(2,1)S(1)} all-gather(bf16[512,192]{0,1:T(8,128)(2,1)S(1)} %copy-done.7), channel_id=1, replica_groups=mesh['expert'=32,'ffn'=4] {'ffn'}, dimensions={1}, use_global_device_ids=true | all-gather | bytes 983040 | tf_op jit(solution)/shard_map/all_gather | solution.py:47
  54.9 3.8 %multiply_convert_fusion.2 = bf16[2048,768]{1,0:T(8,128)(2,1)} fusion(bf16[512,768]{0,1:T(8,128)(2,1)S(1)} %all_gather.7, f32[2048]{0:T(1024)S(1)} %bitcast.108, s32[512]{0:T(512)S(1)} %get-tuple-element.15, s32[512]{0:T(512)S(1)} %get-tuple-element.14), kind=kOutput, calls=%fused_computation.9 | convolution fusion | flops 1616904192 | bytes 3944448 | tf_op jit(solution)/shard_map/dot_general | solution.py:60
  58.6 19.0 %all-to-all-done = bf16[2,32,32,768]{3,2,0,1:T(8,128)(2,1)S(1)} async-done(((bf16[2,32,32,768]{3,2,0,1:T(8,128)(2,1)}), bf16[2,32,32,768]{3,2,0,1:T(8,128)(2,1)S(1)}, u32[]{:S(2)}, u32[]{:S(2)}) %all-to-all-start) | async-done | bytes 3145760 | tf_op jit(solution)/shard_map/all_to_all | solution.py:51
  80.4 5.0 %multiply_convert_fusion.1 = (bf16[2,1024,768]{2,1,0:T(8,128)(2,1)S(1)}, f32[2,1024,768]{2,1,0:T(8,128)}) fusion(bf16[2,1024,768]{2,1,0:T(8,128)(2,1)S(1)} %bitcast.96, bf16[2,768,768]{2,1,0:T(8,128)(2,1)S(1)} %copy-done.11), kind=kOutput, calls=%fused_computation.7 | convolution fusion | flops 2423783424 | bytes 14942208 | tf_op jit(solution)/shard_map/xsd,xdf->xsf/dot_general | solution.py:66
  87.2 2.6 %bitcast_convert_fusion.2 = bf16[768,1024]{1,0:T(8,128)(2,1)} fusion(bf16[2,1024,768]{2,1,0:T(8,128)(2,1)S(1)} %get-tuple-element.22, bf16[2,768,768]{2,1,0:T(8,128)(2,1)S(1)} %copy-done.9), kind=kOutput, calls=%fused_computation.19 | convolution fusion | flops 1208745984 | bytes 4325376 | tf_op jit(solution)/shard_map/fd,sf->ds/dot_general | solution.py:71
  91.7 4.4 %all-to-all-start.1 = ((bf16[2,32,32,768]{3,2,0,1:T(8,128)(2,1)}), bf16[2,32,32,768]{3,2,0,1:T(8,128)(2,1)S(1)}, u32[]{:S(2)}, u32[]{:S(2)}) async-start(bf16[2,32,32,768]{3,2,0,1:T(8,128)(2,1)} %copy.60), calls=%async_computation.3 | async-start | bytes 6291456 | tf_op jit(solution)/shard_map/all_to_all | solution.py:51
  96.3 4.6 %bitcast_convert_fusion.3 = bf16[768,1024]{1,0:T(8,128)(2,1)} fusion(bf16[2,1024,768]{2,1,0:T(8,128)(2,1)} %copy-done.14, bf16[2,768,768]{2,1,0:T(8,128)(2,1)} %param.15), kind=kOutput, calls=%fused_computation.20 | convolution fusion | flops 1208745984 | bytes 4325376 | tf_op jit(solution)/shard_map/fd,sf->ds/dot_general | solution.py:71
  100.8 35.1 %all-to-all-done.1 = bf16[2,32,32,768]{3,2,0,1:T(8,128)(2,1)S(1)} async-done(((bf16[2,32,32,768]{3,2,0,1:T(8,128)(2,1)}), bf16[2,32,32,768]{3,2,0,1:T(8,128)(2,1)S(1)}, u32[]{:S(2)}, u32[]{:S(2)}) %all-to-all-start.1) | async-done | bytes 3145760 | tf_op jit(solution)/shard_map/all_to_all | solution.py:51
  138.8 5.9 %multiply_convert_fusion = bf16[2,1024,768]{2,1,0:T(8,128)(2,1)S(1)} fusion(f32[2,1024,768]{2,1,0:T(8,128)} %get-tuple-element.23, bf16[2,1024,768]{2,1,0:T(8,128)(2,1)S(1)} %bitcast.98, bf16[2,768,768]{2,1,0:T(8,128)(2,1)S(1)} %copy-done.10), kind=kOutput, calls=%fused_computation.6 | convolution fusion | flops 2430074880 | bytes 14942208 | tf_op jit(solution)/shard_map/xsd,xfd->xsf/dot_general | solution.py:110
  149.7 2.8 %bitcast_convert_fusion = bf16[768,1024]{1,0:T(8,128)(2,1)S(1)} fusion(bf16[2,1024,768]{2,1,0:T(8,128)(2,1)} %copy-done.16, bf16[2,768,768]{2,1,0:T(8,128)(2,1)S(1)} %copy-done.13), kind=kOutput, calls=%fused_computation.17 | convolution fusion | flops 1208745984 | bytes 4325376 | tf_op jit(solution)/shard_map/df,sf->ds/dot_general | solution.py:122
  161.2 4.6 %collective-permute-done.3 = bf16[192,1024]{1,0:T(8,128)(2,1)S(1)} collective-permute-done((bf16[192,1024]{1,0:T(8,128)(2,1)S(1)}, bf16[192,1024]{1,0:T(8,128)(2,1)S(1)}, u32[]{:S(2)}, u32[]{:S(2)}) %collective-permute-start.3) | collective-permute-done | bytes 393248 | tf_op jit(solution)/shard_map/ppermute | solution.py:91
  165.9 3.5 %collective-permute-start.4 = (bf16[192,1024]{1,0:T(8,128)(2,1)S(1)}, bf16[192,1024]{1,0:T(8,128)(2,1)S(1)}, u32[]{:S(2)}, u32[]{:S(2)}) collective-permute-start(bf16[192,1024]{1,0:T(8,128)(2,1)S(1)} %fusion.22), channel_id=1, source_target_pairs={{0,3},{1,0},{2,1},{3,2},{4,7},{5,4},{6,5},{7,6},{8,11},{9,8},{10,9... | collective-permute-start | bytes 1179656 | tf_op jit(solution)/shard_map/ppermute | solution.py:91
  172.4 3.8 %collective-permute-done.4 = bf16[192,1024]{1,0:T(8,128)(2,1)S(1)} collective-permute-done((bf16[192,1024]{1,0:T(8,128)(2,1)S(1)}, bf16[192,1024]{1,0:T(8,128)(2,1)S(1)}, u32[]{:S(2)}, u32[]{:S(2)}) %collective-permute-start.4) | collective-permute-done | bytes 393248 | tf_op jit(solution)/shard_map/ppermute | solution.py:91
  177.2 3.4 %collective-permute-start.5 = (bf16[192,1024]{1,0:T(8,128)(2,1)}, bf16[192,1024]{1,0:T(8,128)(2,1)}, u32[]{:S(2)}, u32[]{:S(2)}) collective-permute-start(bf16[192,1024]{1,0:T(8,128)(2,1)} %fusion.21), channel_id=1, source_target_pairs={{0,3},{1,0},{2,1},{3,2},{4,7},{5,4},{6,5},{7,6},{8,11},{9,8},{10,9... | collective-permute-start | bytes 1179656 | tf_op jit(solution)/shard_map/ppermute | solution.py:91
  192.9 7.4 %all-to-all-start.2 = ((bf16[2,192,2,32,32]{1,4,2,0,3:T(8,128)(2,1)}), bf16[2,192,2,32,32]{1,4,2,0,3:T(8,128)(2,1)S(1)}, u32[]{:S(2)}, u32[]{:S(2)}) async-start(bf16[2,192,2,32,32]{1,4,2,0,3:T(8,128)(2,1)} %copy.64), calls=%async_computation.4 | async-start | bytes 4194304 | tf_op jit(solution)/shard_map/all_to_all | solution.py:106
  200.4 7.1 %convolution_convert_fusion.2 = bf16[2,768,768]{2,1,0:T(8,128)(2,1)} fusion(bf16[2,1024,768]{2,1,0:T(8,128)(2,1)} %bitcast.97, bf16[2,1024,768]{2,1,0:T(8,128)(2,1)} %copy-done.16), kind=kOutput, calls=%fused_computation.27 | convolution fusion | flops 2417098752 | bytes 8650752 | tf_op jit(solution)/shard_map/xsd,xsf->xdf/dot_general | solution.py:117
  207.5 4.1 %convolution_convert_fusion.1 = bf16[2,768,768]{2,1,0:T(8,128)(2,1)} fusion(bf16[2,1024,768]{2,1,0:T(8,128)(2,1)S(1)} %copy-done.15, bf16[2,1024,768]{2,1,0:T(8,128)(2,1)S(1)} %bitcast.99), kind=kOutput, calls=%fused_computation.26 | convolution fusion | flops 2417098752 | bytes 8650752 | tf_op jit(solution)/shard_map/xsf,xsd->xfd/dot_general | solution.py:114
  211.6 17.1 %all-to-all-done.2 = bf16[2,192,2,32,32]{1,4,2,0,3:T(8,128)(2,1)S(1)} async-done(((bf16[2,192,2,32,32]{1,4,2,0,3:T(8,128)(2,1)}), bf16[2,192,2,32,32]{1,4,2,0,3:T(8,128)(2,1)S(1)}, u32[]{:S(2)}, u32[]{:S(2)}) %all-to-all-start.2) | async-done | bytes 1572896 | tf_op jit(solution)/shard_map/all_to_all | solution.py:106
  229.1 3.9 %gather_fusion.2 = bf16[1024,192]{1,0:T(8,128)(2,1)S(1)} fusion(bf16[2048,192]{1,0:T(8,128)(2,1)S(1)} %bitcast.94, s32[1024]{0:T(1024)S(1)} %fusion.44), kind=kCustom, calls=%fused_computation.1.clone | custom fusion | bytes 790528 | tf_op jit(solution)/shard_map/jit(_take)/gather | solution.py:133
  233.0 4.9 %gather_fusion.3 = bf16[1024,192]{1,0:T(8,128)(2,1)} fusion(bf16[2048,192]{1,0:T(8,128)(2,1)S(1)} %bitcast.95, s32[1024]{0:T(1024)S(1)} %fusion.44), kind=kCustom, calls=%fused_computation.3.clone | custom fusion | bytes 790528 | tf_op jit(solution)/shard_map/jit(_take)/gather | solution.py:133
  239.8 2.9 %multiply_reduce_fusion = bf16[512,192]{1,0:T(8,128)(2,1)S(1)} fusion(f32[512,2,192]{2,1,0:T(2,128)S(1)} %reshape.163, f32[512,2]{1,0:T(8,128)S(1)} %copy.46), kind=kLoop, calls=%fused_computation.44 | loop fusion | flops 294912 | bytes 987136 | tf_op jit(solution)/shard_map/reduce_sum | solution.py:136
  (98 shorter events, 52.6 us)
Async XLA Ops:
  7.2 3.4 %copy-start.6 = (bf16[512,192]{0,1:T(8,128)(2,1)S(1)}, bf16[512,192]{0,1:T(8,128)(2,1)}, u32[]{:S(2)}) copy-start(bf16[512,192]{0,1:T(8,128)(2,1)} %param.10) | copy-start | bytes 589828
  27.4 10.6 %copy-start.8 = (f32[512,2]{0,1:T(2,128)S(1)}, f32[512,2]{0,1:T(2,128)}, u32[]{:S(2)}) copy-start(f32[512,2]{0,1:T(2,128)} %param.12) | copy-start | bytes 12292
  27.4 50.2 %all-to-all-start = ((bf16[2,32,32,768]{3,2,0,1:T(8,128)(2,1)}), bf16[2,32,32,768]{3,2,0,1:T(8,128)(2,1)S(1)}, u32[]{:S(2)}, u32[]{:S(2)}) async-start(bf16[2,32,32,768]{3,2,0,1:T(8,128)(2,1)} %copy.55), calls=%async_computation | async-start | bytes 6291456 | tf_op jit(solution)/shard_map/all_to_all | solution.py:51
  37.9 142.7 %reduce-scatter.5.cloned.1.call-start = ((), (), s32[]{:S(2)}) async-start(), calls=%async_computation.6 | async-start | bytes 1966080 | tf_op jit(solution)/shard_map/reduce_scatter | solution.py:100
  38.3 3.8 %copy-start.7 = (bf16[512,192]{0,1:T(8,128)(2,1)S(1)}, bf16[512,192]{0,1:T(8,128)(2,1)}, u32[]{:S(2)}) copy-start(bf16[512,192]{0,1:T(8,128)(2,1)} %param.11) | copy-start | bytes 589828
  77.7 2.8 %copy-start.11 = (bf16[2,768,768]{2,1,0:T(8,128)(2,1)S(1)}, bf16[2,768,768]{2,1,0:T(8,128)(2,1)}, u32[]{:S(2)}) copy-start(bf16[2,768,768]{2,1,0:T(8,128)(2,1)} %param.14) | copy-start | bytes 7077892
  77.9 7.5 %copy-start = (bf16[2,32,32,768]{3,2,1,0:T(8,128)(2,1)}, bf16[2,32,32,768]{3,2,1,0:T(8,128)(2,1)S(1)}, u32[]{:S(2)}) copy-start(bf16[2,32,32,768]{3,2,1,0:T(8,128)(2,1)S(1)} %copy.56) | copy-start | bytes 9437188
  80.4 6.7 %copy-start.9 = (bf16[2,768,768]{2,1,0:T(8,128)(2,1)S(1)}, bf16[2,768,768]{2,1,0:T(8,128)(2,1)}, u32[]{:S(2)}) copy-start(bf16[2,768,768]{2,1,0:T(8,128)(2,1)} %param.15) | copy-start | bytes 7077892
  91.7 44.2 %all-to-all-start.1 = ((bf16[2,32,32,768]{3,2,0,1:T(8,128)(2,1)}), bf16[2,32,32,768]{3,2,0,1:T(8,128)(2,1)S(1)}, u32[]{:S(2)}, u32[]{:S(2)}) async-start(bf16[2,32,32,768]{3,2,0,1:T(8,128)(2,1)} %copy.60), calls=%async_computation.3 | async-start | bytes 6291456 | tf_op jit(solution)/shard_map/all_to_all | solution.py:51
  96.1 86.5 %reduce-scatter.3.cloned.1.call-start = ((), (), s32[]{:S(2)}) async-start(), calls=%async_computation.5 | async-start | bytes 1966080 | tf_op jit(solution)/shard_map/reduce_scatter | solution.py:100
  135.9 2.8 %copy-start.10 = (bf16[2,768,768]{2,1,0:T(8,128)(2,1)S(1)}, bf16[2,768,768]{2,1,0:T(8,128)(2,1)}, u32[]{:S(2)}) copy-start(bf16[2,768,768]{2,1,0:T(8,128)(2,1)} %param.15) | copy-start | bytes 7077892
  136.2 8.5 %copy-start.1 = (bf16[2,32,32,768]{3,2,1,0:T(8,128)(2,1)}, bf16[2,32,32,768]{3,2,1,0:T(8,128)(2,1)S(1)}, u32[]{:S(2)}) copy-start(bf16[2,32,32,768]{3,2,1,0:T(8,128)(2,1)S(1)} %copy.61) | copy-start | bytes 9437188
  138.7 5.9 %copy-start.12 = (bf16[2,768,768]{2,1,0:T(8,128)(2,1)S(1)}, bf16[2,768,768]{2,1,0:T(8,128)(2,1)}, u32[]{:S(2)}) copy-start(bf16[2,768,768]{2,1,0:T(8,128)(2,1)} %param.14) | copy-start | bytes 7077892
  148.0 11.8 %collective-permute-start = (bf16[192,1024]{1,0:T(8,128)(2,1)}, bf16[192,1024]{1,0:T(8,128)(2,1)}, u32[]{:S(2)}, u32[]{:S(2)}) collective-permute-start(bf16[192,1024]{1,0:T(8,128)(2,1)} %slice_bitcast_fusion.15), channel_id=1, source_target_pairs={{0,1},{1,2},{2,3},{3,0},{4,5},{5,6},{6,7},{7,4},{8,9},{9,10},{10,1... | collective-permute-start | bytes 1179656 | tf_op jit(solution)/shard_map/ppermute | solution.py:91
  156.0 9.8 %collective-permute-start.3 = (bf16[192,1024]{1,0:T(8,128)(2,1)S(1)}, bf16[192,1024]{1,0:T(8,128)(2,1)S(1)}, u32[]{:S(2)}, u32[]{:S(2)}) collective-permute-start(bf16[192,1024]{1,0:T(8,128)(2,1)S(1)} %slice_bitcast_fusion.11), channel_id=1, source_target_pairs={{0,3},{1,0},{2,1},{3,2},{4,7},{5,4},{6,5},{7,6},{8,11},{9,8},{10,9... | collective-permute-start | bytes 1179656 | tf_op jit(solution)/shard_map/ppermute | solution.py:91
  161.0 10.6 %collective-permute-start.1 = (bf16[192,1024]{1,0:T(8,128)(2,1)S(1)}, bf16[192,1024]{1,0:T(8,128)(2,1)S(1)}, u32[]{:S(2)}, u32[]{:S(2)}) collective-permute-start(bf16[192,1024]{1,0:T(8,128)(2,1)S(1)} %fusion.25), channel_id=1, source_target_pairs={{0,1},{1,2},{2,3},{3,0},{4,5},{5,6},{6,7},{7,4},{8,9},{9,10},{10,1... | collective-permute-start | bytes 1179656 | tf_op jit(solution)/shard_map/ppermute | solution.py:91
  165.9 10.4 %collective-permute-start.4 = (bf16[192,1024]{1,0:T(8,128)(2,1)S(1)}, bf16[192,1024]{1,0:T(8,128)(2,1)S(1)}, u32[]{:S(2)}, u32[]{:S(2)}) collective-permute-start(bf16[192,1024]{1,0:T(8,128)(2,1)S(1)} %fusion.22), channel_id=1, source_target_pairs={{0,3},{1,0},{2,1},{3,2},{4,7},{5,4},{6,5},{7,6},{8,11},{9,8},{10,9... | collective-permute-start | bytes 1179656 | tf_op jit(solution)/shard_map/ppermute | solution.py:91
  172.4 12.1 %collective-permute-start.2 = (bf16[192,1024]{1,0:T(8,128)(2,1)}, bf16[192,1024]{1,0:T(8,128)(2,1)}, u32[]{:S(2)}, u32[]{:S(2)}) collective-permute-start(bf16[192,1024]{1,0:T(8,128)(2,1)} %fusion.24), channel_id=1, source_target_pairs={{0,1},{1,2},{2,3},{3,0},{4,5},{5,6},{6,7},{7,4},{8,9},{9,10},{10,1... | collective-permute-start | bytes 1179656 | tf_op jit(solution)/shard_map/ppermute | solution.py:91
  177.2 10.6 %collective-permute-start.5 = (bf16[192,1024]{1,0:T(8,128)(2,1)}, bf16[192,1024]{1,0:T(8,128)(2,1)}, u32[]{:S(2)}, u32[]{:S(2)}) collective-permute-start(bf16[192,1024]{1,0:T(8,128)(2,1)} %fusion.21), channel_id=1, source_target_pairs={{0,3},{1,0},{2,1},{3,2},{4,7},{5,4},{6,5},{7,6},{8,11},{9,8},{10,9... | collective-permute-start | bytes 1179656 | tf_op jit(solution)/shard_map/ppermute | solution.py:91
  186.5 4.4 %copy-start.4 = (bf16[192,1024]{0,1:T(8,128)(2,1)S(1)}, bf16[192,1024]{0,1:T(8,128)(2,1)}, u32[]{:S(2)}) copy-start(bf16[192,1024]{0,1:T(8,128)(2,1)} %copy.59) | copy-start | bytes 1179652
  186.5 4.4 %copy-start.5 = (bf16[192,1024]{0,1:T(8,128)(2,1)S(1)}, bf16[192,1024]{0,1:T(8,128)(2,1)}, u32[]{:S(2)}) copy-start(bf16[192,1024]{0,1:T(8,128)(2,1)} %copy.58) | copy-start | bytes 1179652
  192.9 35.8 %all-to-all-start.2 = ((bf16[2,192,2,32,32]{1,4,2,0,3:T(8,128)(2,1)}), bf16[2,192,2,32,32]{1,4,2,0,3:T(8,128)(2,1)S(1)}, u32[]{:S(2)}, u32[]{:S(2)}) async-start(bf16[2,192,2,32,32]{1,4,2,0,3:T(8,128)(2,1)} %copy.64), calls=%async_computation.4 | async-start | bytes 4194304 | tf_op jit(solution)/shard_map/all_to_all | solution.py:106
  200.4 7.1 %copy-start.2 = (bf16[2,32,32,768]{3,2,1,0:T(8,128)(2,1)S(1)}, bf16[2,32,32,768]{3,2,1,0:T(8,128)(2,1)}, u32[]{:S(2)}) copy-start(bf16[2,32,32,768]{3,2,1,0:T(8,128)(2,1)} %copy-done.1) | copy-start | bytes 9437188
  200.4 7.1 %copy-start.15 = (bf16[2,1024,768]{2,1,0:T(8,128)(2,1)S(1)}, bf16[2,1024,768]{2,1,0:T(8,128)(2,1)}, u32[]{:S(2)}) copy-start(bf16[2,1024,768]{2,1,0:T(8,128)(2,1)} %copy-done.14) | copy-start | bytes 9437188
  (4 other events, 8.7 us)
Sparse Core Ops, SparseCore 0:
  89.9 22.9 reduce-scatter.4
  115.3 25.3 reduce-scatter.2
